TPU v7x, 32 devices: a whole 2x2x4 slice. The times are simulated.
32 devices in a mesh: seq: 8 (over z, x), tp: 4 (over y, core).
Axes of the slice: x: 2, y: 2, z: 4, core: 2. Of those that a mesh axis runs over, the one named last changes fastest.
Arguments:
- queries: bfloat16 [1024, 4096], P('seq', 'tp'), may hold values from -600 to 600
- suffix_keys: bfloat16 [1024, 1024], P('seq', 'tp'), may hold values from -6 to 6
- suffix_values: bfloat16 [1024, 1024], P('seq', 'tp'), may hold values from -6 to 6
- prefix_keys: bfloat16 [512, 1024], P('seq', 'tp'), may hold values from -6 to 6
- prefix_values: bfloat16 [512, 1024], P('seq', 'tp'), may hold values from -6 to 6
- suffix_lengths: int32 [24], replicated, may hold values from 1 to 128, 1024 in all
- request_group: int32 [24], replicated, may hold values from 0 to 3
- block_group: int32 [8], replicated, may hold values from 0 to 3, as said below
Outputs:
- attended: bfloat16 [1024, 4096], P('seq', 'tp')
- cache_keys: bfloat16 [1024, 1024], P(('seq', 'tp'))
- cache_values: bfloat16 [1024, 1024], P(('seq', 'tp'))
Inputs may be any that keep to these rules, and one draw needn't show every extreme that they name: `suffix_lengths`: the suffixes fill the 1024 packed tokens end to end in order; the longest has exactly 128 tokens. `block_group`: each prefix is held by exactly 2 blocks, in any order.
All inputs are finite; a program needn't handle non-finite values.
Results may differ from a plain program's by a relative error of at most 0.009.
The roundings to bfloat16 on the way count: a program that leaves them out, or rounds other values in their place, can miss the bound.
Values may be sent and summed in bfloat16 or wider, within the bound.
No kernel may reach another device: no remote copies, remote signals or barrier semaphores. Data moves between devices by JAX's collectives and lax.ppermute only.
A program may use at most 64 MiB of HBM per device.

v0:
```python
import math
import jax
import jax.numpy as jnp
from jax import lax
from jax.sharding import PartitionSpec as P

HD = 128
GROUPS = 4
BIG_NEGATIVE = -1e30


def from_behind(array, axis, by):
    length = lax.axis_size(axis)
    pairs = [(i, i + by) for i in range(length) if 0 <= i + by < length]
    return lax.ppermute(array, axis, pairs)


def rotate(values, position):
    half = values.shape[-1] // 2
    freq = jnp.exp(
        jnp.arange(half, dtype=jnp.float32) * (-2.0 * math.log(500000.0) / values.shape[-1])
    )
    angle = position.astype(jnp.float32)[:, None] * freq[None, :]
    cosine = jnp.cos(angle)[:, None, :]
    sine = jnp.sin(angle)[:, None, :]
    floats = values.astype(jnp.float32)
    lower = floats[..., :half]
    upper = floats[..., half:]
    return jnp.concatenate(
        [lower * cosine - upper * sine, upper * cosine + lower * sine], axis=-1
    ).astype(jnp.bfloat16)


def token_info(index, suffix_lengths, request_group):
    ends = jnp.cumsum(suffix_lengths)
    request = jnp.sum((index[:, None] >= ends[None, :]).astype(jnp.int32), axis=1)
    onehot = request[:, None] == jnp.arange(suffix_lengths.shape[0], dtype=jnp.int32)[None, :]
    first = jnp.sum(jnp.where(onehot, (ends - suffix_lengths)[None, :], 0), axis=1)
    group = jnp.sum(jnp.where(onehot, request_group[None, :], 0), axis=1)
    return (request, index - first, group)


def body(
    queries,
    suffix_keys,
    suffix_values,
    prefix_keys,
    prefix_values,
    suffix_lengths,
    request_group,
    block_group,
):
    rows = queries.shape[0]
    kv_cols = suffix_keys.shape[1]
    kv_heads = kv_cols // HD
    q_heads = queries.shape[1] // HD
    repeat = q_heads // kv_heads
    devices = lax.axis_size("seq")
    me = lax.axis_index("seq")
    block_rows = prefix_keys.shape[0]
    prefix_len = block_rows * devices // GROUPS
    span = max(1, min(2048 // rows, devices // 8))
    scale = HD ** (-0.5)
    index = me * rows + jnp.arange(rows, dtype=jnp.int32)
    request, offset, group = token_info(index, suffix_lengths, request_group)
    position = offset + prefix_len
    q_rot = rotate(queries.reshape(rows, q_heads, HD), position).reshape(rows, kv_heads, repeat, HD)
    k_rot = rotate(suffix_keys.reshape(rows, kv_heads, HD), position).reshape(rows, kv_cols)

    def update(carry, keys, values, visible):
        high, total, accum = carry
        keys_split = keys.reshape(keys.shape[0], kv_heads, HD)
        values_split = values.reshape(values.shape[0], kv_heads, HD)
        scores = (
            jnp.einsum("bgrd,kgd->bgrk", q_rot, keys_split, preferred_element_type=jnp.float32)
            * scale
        )
        mask = visible[:, None, None, :]
        scores = jnp.where(mask, scores, BIG_NEGATIVE)
        new_high = jnp.maximum(high, jnp.max(scores, axis=-1))
        weights = jnp.where(mask, jnp.exp(scores - new_high[..., None]), 0.0)
        factor = jnp.exp(high - new_high)
        total = total * factor + jnp.sum(weights, axis=-1)
        accum = accum * factor[..., None] + jnp.einsum(
            "bgrk,kgd->bgrd",
            weights.astype(jnp.bfloat16),
            values_split,
            preferred_element_type=jnp.float32,
        )
        return (new_high, total, accum)

    def guarded(carry, keys, values, visible):
        return update(carry, keys, values, visible)

    def suffix_visible(back):
        key_index = (me - back) * rows + jnp.arange(rows, dtype=jnp.int32)
        key_request, _, _ = token_info(key_index, suffix_lengths, request_group)
        return (
            (key_index[None, :] >= 0)
            & (key_request[None, :] == request[:, None])
            & (key_index[None, :] <= index[:, None])
        )

    start_state = (
        jnp.full((rows, kv_heads, repeat), BIG_NEGATIVE, jnp.float32),
        jnp.zeros((rows, kv_heads, repeat), jnp.float32),
        jnp.zeros((rows, kv_heads, repeat, HD), jnp.float32),
    )
    carry = start_state
    keys = lax.all_gather(prefix_keys, "seq", axis=0, tiled=True)
    values = lax.all_gather(prefix_values, "seq", axis=0, tiled=True)
    count = keys.shape[0]
    width = 512

    def one_step(state, step):
        first = step * width
        keys_part = lax.dynamic_slice_in_dim(keys, first, width, 0)
        values_part = lax.dynamic_slice_in_dim(values, first, width, 0)
        row_index = first + jnp.arange(width, dtype=jnp.int32)
        holder = row_index // block_rows
        matches = holder[:, None] == jnp.arange(block_group.shape[0], dtype=jnp.int32)[None, :]
        row_group = jnp.sum(jnp.where(matches, block_group[None, :], 0), axis=1)
        visible = row_group[None, :] == group[:, None]
        return (guarded(state, keys_part, values_part, visible), None)

    carry, _ = lax.scan(one_step, carry, jnp.arange(count // width, dtype=jnp.int32))
    carry = guarded(carry, k_rot, suffix_values, suffix_visible(0))
    for back in range(1, span + 1):
        earlier_keys, earlier_values = from_behind((k_rot, suffix_values), "seq", back)
        carry = guarded(carry, earlier_keys, earlier_values, suffix_visible(back))
    high, total, accum = carry
    attended = (accum / total[..., None]).reshape(rows, q_heads * HD).astype(jnp.bfloat16)
    cache_keys, cache_values = (
        lax.all_to_all(k_rot, "tp", split_axis=0, concat_axis=1, tiled=True),
        lax.all_to_all(suffix_values, "tp", split_axis=0, concat_axis=1, tiled=True),
    )
    return (attended, cache_keys, cache_values)


def solution(mesh):
    return jax.shard_map(
        body,
        mesh=mesh,
        in_specs=(
            P("seq", "tp"),
            P("seq", "tp"),
            P("seq", "tp"),
            P("seq", "tp"),
            P("seq", "tp"),
            P(),
            P(),
            P(),
        ),
        out_specs=(P("seq", "tp"), P(("seq", "tp"), None), P(("seq", "tp"), None)),
        check_vma=False,
    )
```

profile of v0, /device:TPU:0, one launch (start us, length us, event | category | flops | bytes accessed | tf_op | source)
XLA Modules:
  0.0 101.6 jit_solution(3033059807300362979)
XLA Ops:
  0.7 0.8 copy.95
  1.5 0.1 reduce
  1.6 0.7 sub.87
  2.3 0.1 convert_reduce_fusion
  2.4 0.7 select_reduce_fusion.2
  3.1 0.9 copy.101
  4.1 0.1 copy.129
  4.2 0.1 copy.130
  4.3 0.3 multiply_cosine_fusion
  4.7 0.1 maximum_convert_fusion
  4.7 0.7 copy.106
  5.5 5.5 %collective-permute-start = (bf16[128,256]{0,1:T(8,128)(2,1)}, bf16[128,256]{0,1:T(8,128)(2,1)}, u32[]{:S(2)}, u32[]{:S(2)}) collective-permute-start(bf16[128,256]{0,1:T(8,128)(2,1)} %bitcast.19), channel_id=1, source_target_pairs={{0,4},{4,8},{8,12},{12,16},{16,20},{20,24},{24,28},{1,5},{5,9},{9,... | collective-permute-start | bytes 196616 | tf_op jit(solution)/shard_map/ppermute | solution.py:15
  10.9 3.5 %collective-permute-start.1 = (bf16[128,256]{1,0:T(8,128)(2,1)}, bf16[128,256]{1,0:T(8,128)(2,1)}, u32[]{:S(2)}, u32[]{:S(2)}) collective-permute-start(bf16[128,256]{1,0:T(8,128)(2,1)} %param.10), channel_id=1, source_target_pairs={{0,4},{4,8},{8,12},{12,16},{16,20},{20,24},{24,28},{1,5},{5,9},{9,... | collective-permute-start | bytes 196616 | tf_op jit(solution)/shard_map/ppermute | solution.py:15
  14.4 0.1 copy.110
  14.5 0.0 copy-start.7
  14.5 0.7 convert_element_type.70
  15.2 3.3 %all-to-all-start = ((bf16[4,32,256]{2,1,0:T(8,128)(2,1)}), bf16[4,32,256]{2,1,0:T(8,128)(2,1)S(1)}, u32[]{:S(2)}, u32[]{:S(2)}) async-start(bf16[4,32,256]{2,1,0:T(8,128)(2,1)} %convert_element_type.70), calls=%async_computation | async-start | bytes 131072 | tf_op jit(solution)/shard_map/all_to_all | solution.py:134
  18.5 0.1 copy.133
  18.6 0.0 copy-start.8
  18.7 0.2 fusion.46
  18.9 31.0 %all_gather.6 = bf16[512,256]{1,0:T(8,128)(2,1)S(1)} all-gather(bf16[64,256]{1,0:T(8,128)(2,1)S(1)} %copy-done.7), channel_id=1, replica_groups=mesh['seq'=8,'tp'=4] {'seq'}, dimensions={0}, use_global_device_ids=true | all-gather | bytes 294912 | tf_op jit(solution)/shard_map/all_gather | solution.py:110
  49.8 0.1 copy.98
  50.0 0.2 subtract_convert_fusion
  50.2 0.1 select_reduce_fusion
  50.3 0.1 broadcast_compare_fusion
  50.4 0.8 compare_and_fusion
  51.2 1.2 %bitcast_reduce_fusion = (f32[128,2,4]{0,2,1:T(4,128)}, f32[2,128,4,512]{3,1,2,0:T(8,128)S(1)}) fusion(pred[128,512]{1,0:T(8,128)(4,1)S(1)} %broadcast_compare_fusion, bf16[512,2,128,1]{0,2,3,1:T(8,128)(2,1)S(1)} %bitcast.101, bf16[128,2,4,64]{3,0,2,1:T(8,128)(2,1)S(1)} %bitcast.98, bf16[128,2,4,64]{3,0,2,1:T(8,128)(2,1)S(1)} %bitcast.95), kind=kOutput, calls=%fused_computation.1 | convolution fusion | flops 136313856 | bytes 2691072 | tf_op jit(solution)/shard_map/while/body/eval_jaxpr/bgrd,kgd->bgrk/dot_general | solution.py:75
  52.4 0.9 fusion.49
  53.3 0.6 copy-done.4
  53.9 3.9 %all-to-all-start.1 = ((bf16[4,32,256]{2,1,0:T(8,128)(2,1)}), bf16[4,32,256]{2,1,0:T(8,128)(2,1)}, u32[]{:S(2)}, u32[]{:S(2)}) async-start(bf16[4,32,256]{2,1,0:T(8,128)(2,1)} %bitcast.29), calls=%async_computation.1 | async-start | bytes 131072 | tf_op jit(solution)/shard_map/all_to_all | solution.py:135
  57.8 31.0 %all_gather.7 = bf16[512,256]{1,0:T(8,128)(2,1)S(1)} all-gather(bf16[64,256]{1,0:T(8,128)(2,1)} %param.12), channel_id=1, replica_groups=mesh['seq'=8,'tp'=4] {'seq'}, dimensions={0}, use_global_device_ids=true | all-gather | bytes 294912 | tf_op jit(solution)/shard_map/all_gather | solution.py:111
  88.9 0.9 copy.124
  89.8 0.8 copy.100
  90.7 1.5 %copy.131 = bf16[4,4,8,256]{3,2,0,1:T(8,128)(2,1)} copy(bf16[4,4,8,256]{3,2,1,0:T(8,128)(2,1)} %bitcast.106) | data formatting | bytes 131072 | tf_op jit(solution)/shard_map/all_to_all | solution.py:134
  92.2 1.5 %copy.132 = bf16[4,4,8,256]{3,2,0,1:T(8,128)(2,1)} copy(bf16[4,4,8,256]{3,2,1,0:T(8,128)(2,1)} %bitcast.46) | data formatting | bytes 131072 | tf_op jit(solution)/shard_map/all_to_all | solution.py:135
  93.6 0.0 collective-permute-done
  93.6 1.2 %fusion.48 = (f32[128,2,4]{0,2,1:T(4,128)S(1)}, f32[128,2,4,128]{0,3,2,1:T(8,128)S(1)}) fusion(bf16[128,2,128,1]{0,2,3,1:T(8,128)(2,1)} %bitcast.39, bf16[128,2,4,64]{3,0,2,1:T(8,128)(2,1)S(1)} %bitcast.100, bf16[128,2,4,64]{3,0,2,1:T(8,128)(2,1)S(1)} %bitcast.97, pred[128,128]{0,1:T(8,128)(4,1)} %get-tuple-element.67), kind=kOutput, calls=%fused_computation.88 | convolution fusion | flops 34470912 | bytes 872448 | tf_op jit(solution)/shard_map/bgrd,kgd->bgrk/dot_general | solution.py:75
  94.9 0.7 fusion.44
  95.6 0.1 fusion.21
  95.7 0.0 copy-start.3
  95.7 0.2 convolution_bitcast_fusion.1
  96.0 0.7 fusion.2
  96.7 0.1 fusion.23
  96.9 1.6 %fusion.7 = f32[128,2,4,128]{0,3,2,1:T(8,128)} fusion(f32[128,2,4,128]{0,3,2,1:T(8,128)S(1)} %convolution_bitcast_fusion.1, bf16[512,2,128,1]{0,2,3,1:T(8,128)(2,1)S(1)} %bitcast.104, f32[2,128,4,512]{3,1,2,0:T(8,128)S(1)} %get-tuple-element.76, f32[128,2,4]{0,2,1:T(4,128)S(1)} %get-tuple-element.66, pred[128,512]{1,0:T(8,128)(4,1)S(1)} %broadcast_compare_fusion, ...), kind=kOutput, calls=%fused_computation.13 | convolution fusion | flops 137363456 | bytes 3489792 | tf_op jit(solution)/shard_map/while/body/eval_jaxpr/bgrk,kgd->bgrd/dot_general | solution.py:84
  98.5 0.0 collective-permute-done.1
  98.5 0.9 copy.108
  99.4 1.3 %fusion.14 = bf16[128,2,4,128]{0,3,2,1:T(8,128)(2,1)S(1)} fusion(f32[128,2,4,128]{0,3,2,1:T(8,128)} %fusion.7, bf16[128,2,128,1]{0,2,3,1:T(8,128)(2,1)S(1)} %bitcast.109, f32[128,2,4,128]{0,3,2,1:T(8,128)S(1)} %copy-done.1, f32[128,2,4]{0,2,1:T(4,128)S(1)} %get-tuple-element.52, f32[128,2,4]{0,2,1:T(4,128)S(1)} %get-tuple-element.55, ...), kind=kOutput, calls=%fused_computation.22 | convolution fusion | flops 34340864 | bytes 1400832 | tf_op jit(solution)/shard_map/bgrk,kgd->bgrd/dot_general | solution.py:84
  100.7 0.9 copy.113
  (26 shorter events, 0.2 us)
Async XLA Ops:
  0.6 17.9 %copy-start.2 = (bf16[128,1024]{1,0:T(8,128)(2,1)S(1)}, bf16[128,1024]{1,0:T(8,128)(2,1)}, u32[]{:S(2)}) copy-start(bf16[128,1024]{1,0:T(8,128)(2,1)} %param.8) | copy-start | bytes 786436
  5.5 88.2 %collective-permute-start = (bf16[128,256]{0,1:T(8,128)(2,1)}, bf16[128,256]{0,1:T(8,128)(2,1)}, u32[]{:S(2)}, u32[]{:S(2)}) collective-permute-start(bf16[128,256]{0,1:T(8,128)(2,1)} %bitcast.19), channel_id=1, source_target_pairs={{0,4},{4,8},{8,12},{12,16},{16,20},{20,24},{24,28},{1,5},{5,9},{9,... | collective-permute-start | bytes 196616 | tf_op jit(solution)/shard_map/ppermute | solution.py:15
  10.9 87.5 %collective-permute-start.1 = (bf16[128,256]{1,0:T(8,128)(2,1)}, bf16[128,256]{1,0:T(8,128)(2,1)}, u32[]{:S(2)}, u32[]{:S(2)}) collective-permute-start(bf16[128,256]{1,0:T(8,128)(2,1)} %param.10), channel_id=1, source_target_pairs={{0,4},{4,8},{8,12},{12,16},{16,20},{20,24},{24,28},{1,5},{5,9},{9,... | collective-permute-start | bytes 196616 | tf_op jit(solution)/shard_map/ppermute | solution.py:15
  14.5 4.4 %copy-start.7 = (bf16[64,256]{1,0:T(8,128)(2,1)S(1)}, bf16[64,256]{1,0:T(8,128)(2,1)}, u32[]{:S(2)}) copy-start(bf16[64,256]{1,0:T(8,128)(2,1)} %param.11) | copy-start | bytes 98308
  15.2 38.1 %all-to-all-start = ((bf16[4,32,256]{2,1,0:T(8,128)(2,1)}), bf16[4,32,256]{2,1,0:T(8,128)(2,1)S(1)}, u32[]{:S(2)}, u32[]{:S(2)}) async-start(bf16[4,32,256]{2,1,0:T(8,128)(2,1)} %convert_element_type.70), calls=%async_computation | async-start | bytes 131072 | tf_op jit(solution)/shard_map/all_to_all | solution.py:134
  18.6 31.6 %copy-start.8 = (s32[8]{0:T(128)S(1)}, s32[8]{0:T(128)}, u32[]{:S(2)}) copy-start(s32[8]{0:T(128)} %param.15) | copy-start | bytes 100
  53.3 0.6 copy-start.4
  53.9 38.2 %all-to-all-start.1 = ((bf16[4,32,256]{2,1,0:T(8,128)(2,1)}), bf16[4,32,256]{2,1,0:T(8,128)(2,1)}, u32[]{:S(2)}, u32[]{:S(2)}) async-start(bf16[4,32,256]{2,1,0:T(8,128)(2,1)} %bitcast.29), calls=%async_computation.1 | async-start | bytes 131072 | tf_op jit(solution)/shard_map/all_to_all | solution.py:135
  94.9 2.0 %copy-start = (f32[128,2,4,128]{0,3,2,1:T(8,128)}, f32[128,2,4,128]{0,3,2,1:T(8,128)S(1)}, u32[]{:S(2)}) copy-start(f32[128,2,4,128]{0,3,2,1:T(8,128)S(1)} %get-tuple-element.72) | copy-start | bytes 1572868
  94.9 1.8 %copy-start.5 = (pred[128,128]{0,1:T(8,128)(4,1)S(1)}, pred[128,128]{0,1:T(8,128)(4,1)}, u32[]{:S(2)}) copy-start(pred[128,128]{0,1:T(8,128)(4,1)} %get-tuple-element.67) | copy-start | bytes 49156
  95.7 1.1 %copy-start.6 = (f32[128,2,4]{0,2,1:T(4,128)S(1)}, f32[128,2,4]{0,2,1:T(4,128)}, u32[]{:S(2)}) copy-start(f32[128,2,4]{0,2,1:T(4,128)} %get-tuple-element.75) | copy-start | bytes 12292
  95.7 1.1 %copy-start.3 = (bf16[512,256]{0,1:T(8,128)(2,1)S(1)}, bf16[512,256]{0,1:T(8,128)(2,1)}, u32[]{:S(2)}) copy-start(bf16[512,256]{0,1:T(8,128)(2,1)} %copy.100) | copy-start | bytes 786436
  96.9 2.6 %copy-start.1 = (f32[128,2,4,128]{0,3,2,1:T(8,128)S(1)}, f32[128,2,4,128]{0,3,2,1:T(8,128)}, u32[]{:S(2)}) copy-start(f32[128,2,4,128]{0,3,2,1:T(8,128)} %copy-done) | copy-start | bytes 1572868
where the time goes:
time: 102 us
  blocking collectives  62 us (61%)
  starting transfers between devices  16.1 us (16%)
  local copies, waits for them, and re-layouts  11.1 us (11%)
  matrix products  6.46 us (6%)
  other arithmetic  5.01 us (5%)
    all_gather x1, blocking collectives, body(): values = lax.all_gather(prefix_values, 'seq', axis=0, tiled=True)  31 us
    all_gather x1, blocking collectives, body(): keys = lax.all_gather(prefix_keys, 'seq', axis=0, tiled=True)  31 us
    ppermute x2, starting transfers between devices, from_behind(): return lax.ppermute(array, axis, pairs)  8.92 us
    all_to_all x1, starting transfers between devices, body(): lax.all_to_all(suffix_values, 'tp', split_axis=0, concat_axis=1, tiled=True)  3.89 us
    dot_general x3, matrix products, update(): jnp.einsum('bgrd,kgd->bgrk', q_rot, keys_split, preferred_element_type=jn...  3.34 us
    all_to_all x1, starting transfers between devices, body(): lax.all_to_all(k_rot, 'tp', split_axis=0, concat_axis=1, tiled=True)  3.28 us
    dot_general x3, matrix products, update(): jnp.einsum('bgrk,kgd->bgrd', weights.astype(jnp.bfloat16), values_split,...  3.12 us
    unnamed x23, local copies, waits for them, and re-layouts  2.76 us
  transfers between devices with their start and end apart: 4, of which 0 were waited for; matrix products, arithmetic and copies ran while one was open for 14% of the time, Pallas kernels for 0%

commit v1 on v0

--- a/solution.py
+++ b/solution.py
@@ -108,7 +108,19 @@
     )
     carry = start_state
     keys = lax.all_gather(prefix_keys, "seq", axis=0, tiled=True)
-    values = lax.all_gather(prefix_values, "seq", axis=0, tiled=True)
+    lanes = lax.axis_size("seq")
+    buffer = [(idx, (idx + 1) % lanes) for idx in range(lanes)]
+    so_far_all = [(idx, (idx - 1) % lanes) for idx in range(lanes)]
+    o_now, a_next = ([prefix_values], [prefix_values])
+    for _ in range(lanes // 2):
+        outer = lax.ppermute(o_now[-1], "seq", buffer)
+        o_now.append(outer)
+    for _ in tuple(range((lanes - 1) // 2)):
+        next_value = lax.ppermute(a_next[-1], "seq", so_far_all)
+        a_next.append(next_value)
+    arr_next = jnp.concatenate([*o_now[::-1], *a_next[1:]], axis=0)
+    latest = lax.axis_index("seq")
+    values = jnp.roll(arr_next, shift=(latest - lanes // 2) * prefix_values.shape[0], axis=0)
     count = keys.shape[0]
     width = 512
 

time: 102 us -> 95.2 us (0.933)
  blocking collectives: 62 us -> 31.2 us
  starting transfers between devices: 16.1 us -> 28 us
  waiting for transfers between devices: 0.01 us -> 8.52 us
  local copies, waits for them, and re-layouts: 11.1 us -> 14.2 us
    all_gather x1 -> x0, blocking collectives: 31 us -> none  [body(): values = lax.all_gather(prefix_values, 'seq', axis=0, tiled=True)]
    ppermute x0 -> x7, starting transfers between devices: none -> 15.7 us  [the longest x3 12.6 us: body(): next_value = lax.ppermute(a_next[-1], 'seq', so_far_all)]
    ppermute x0 -> x7, waiting for transfers between devices: none -> 8.51 us  [the longest x4 8.5 us: body(): outer = lax.ppermute(o_now[-1], 'seq', buffer)]
    unnamed x23 -> x36, local copies, waits for them, and re-layouts: 2.76 us -> 8.53 us
    ppermute x2, starting transfers between devices: 8.92 us -> 5.8 us  [from_behind(): return lax.ppermute(array, axis, pairs)]
    dot_general x3, matrix products: 3.34 us -> 2.31 us  [update(): jnp.einsum('bgrd,kgd->bgrk', q_rot, keys_split, preferred_element_type=jn...]
  transfers between devices with their start and end apart: 4 -> 11, of which waited for: 0 -> 2; matrix products, arithmetic and copies ran while one was open for 14% -> 20% of each run, Pallas kernels for 0% -> 0%
where the time goes in v1:
time: 95.2 us; the launch traced here: 94.1 us
  blocking collectives  31.2 us (33%)
  starting transfers between devices  28 us (29%)
  local copies, waits for them, and re-layouts  14.2 us (15%)
  waiting for transfers between devices  8.52 us (9%)
  matrix products  6.27 us (7%)
  other arithmetic  4.87 us (5%)
  between operations  0.98 us (1%)
    all_gather x1, blocking collectives, body(): keys = lax.all_gather(prefix_keys, 'seq', axis=0, tiled=True)  31.2 us
    ppermute x3, starting transfers between devices, body(): next_value = lax.ppermute(a_next[-1], 'seq', so_far_all)  12.6 us
    unnamed x36, local copies, waits for them, and re-layouts  8.53 us
    ppermute x4, waiting for transfers between devices, body(): outer = lax.ppermute(o_now[-1], 'seq', buffer)  8.5 us
    ppermute x2, starting transfers between devices, from_behind(): return lax.ppermute(array, axis, pairs)  5.8 us
    dot_general x3, matrix products, update(): jnp.einsum('bgrk,kgd->bgrd', weights.astype(jnp.bfloat16), values_split,...  3.96 us
    all_to_all x1, starting transfers between devices, body(): lax.all_to_all(k_rot, 'tp', split_axis=0, concat_axis=1, tiled=True)  3.29 us
    all_to_all x1, starting transfers between devices, body(): lax.all_to_all(suffix_values, 'tp', split_axis=0, concat_axis=1, tiled=True)  3.29 us
  transfers between devices with their start and end apart: 11, of which 2 were waited for; matrix products, arithmetic and copies ran while one was open for 20% of the time, Pallas kernels for 0%

profile of v1, /device:TPU:0, one launch (start us, length us, event | category | flops | bytes accessed | tf_op | source)
XLA Modules:
  0.0 94.1 jit_solution(5587068092609812729)
XLA Ops:
  0.6 3.0 %collective-permute-start = (bf16[64,256]{1,0:T(8,128)(2,1)}, bf16[64,256]{1,0:T(8,128)(2,1)}, u32[]{:S(2)}, u32[]{:S(2)}) collective-permute-start(bf16[64,256]{1,0:T(8,128)(2,1)} %param.12), channel_id=1, source_target_pairs={{0,4},{4,8},{8,12},{12,16},{16,20},{20,24},{24,28},{28,0},{1,5},{5... | collective-permute-start | bytes 98312 | tf_op jit(solution)/shard_map/ppermute | solution.py:116
  3.6 3.1 %collective-permute-start.4 = (bf16[64,256]{1,0:T(8,128)(2,1)}, bf16[64,256]{1,0:T(8,128)(2,1)}, u32[]{:S(2)}, u32[]{:S(2)}) collective-permute-start(bf16[64,256]{1,0:T(8,128)(2,1)} %param.12), channel_id=1, source_target_pairs={{0,28},{4,0},{8,4},{12,8},{16,12},{20,16},{24,20},{28,24},{1,29},{... | collective-permute-start | bytes 98312 | tf_op jit(solution)/shard_map/ppermute | solution.py:119
  6.7 1.9 %collective-permute-start.8 = (bf16[128,256]{1,0:T(8,128)(2,1)}, bf16[128,256]{1,0:T(8,128)(2,1)}, u32[]{:S(2)}, u32[]{:S(2)}) collective-permute-start(bf16[128,256]{1,0:T(8,128)(2,1)} %param.10), channel_id=1, source_target_pairs={{0,4},{4,8},{8,12},{12,16},{16,20},{20,24},{24,28},{1,5},{5,9},{9,... | collective-permute-start | bytes 196616 | tf_op jit(solution)/shard_map/ppermute | solution.py:15
  8.6 3.3 %all-to-all-start.1 = ((bf16[4,32,256]{2,1,0:T(8,128)(2,1)}), bf16[4,32,256]{2,1,0:T(8,128)(2,1)S(1)}, u32[]{:S(2)}, u32[]{:S(2)}) async-start(bf16[4,32,256]{2,1,0:T(8,128)(2,1)} %bitcast.107), calls=%async_computation.1 | async-start | bytes 131072 | tf_op jit(solution)/shard_map/all_to_all | solution.py:147
  12.0 0.7 copy.95
  12.7 0.1 reduce
  12.9 0.7 sub.94
  13.6 0.7 select_reduce_fusion.2
  14.4 0.9 %copy.101 = bf16[128,256]{0,1:T(8,128)(2,1)S(1)} copy(bf16[128,256]{1,0:T(8,128)(2,1)} %param.9) | data formatting | bytes 131072 | tf_op args[1]
  15.6 0.3 multiply_cosine_fusion
  16.0 0.7 copy.106
  16.7 3.9 %collective-permute-start.7 = (bf16[128,256]{0,1:T(8,128)(2,1)}, bf16[128,256]{0,1:T(8,128)(2,1)}, u32[]{:S(2)}, u32[]{:S(2)}) collective-permute-start(bf16[128,256]{0,1:T(8,128)(2,1)} %bitcast.19), channel_id=1, source_target_pairs={{0,4},{4,8},{8,12},{12,16},{16,20},{20,24},{24,28},{1,5},{5,9},{9,... | collective-permute-start | bytes 196616 | tf_op jit(solution)/shard_map/ppermute | solution.py:15
  20.6 31.2 %all_gather.3 = bf16[512,256]{1,0:T(8,128)(2,1)S(1)} all-gather(bf16[64,256]{1,0:T(8,128)(2,1)} %param.11), channel_id=1, replica_groups=mesh['seq'=8,'tp'=4] {'seq'}, dimensions={0}, use_global_device_ids=true | all-gather | bytes 294912 | tf_op jit(solution)/shard_map/all_gather | solution.py:110
  51.9 0.1 copy.98
  52.2 0.2 fusion.46
  52.4 0.3 copy-done.7
  52.9 0.2 subtract_convert_fusion
  53.1 0.6 bitcast_reduce_fusion
  53.8 0.2 compare_and_fusion.1
  54.0 0.7 convert_element_type.70
  54.7 3.3 %all-to-all-start = ((bf16[4,32,256]{2,1,0:T(8,128)(2,1)}), bf16[4,32,256]{2,1,0:T(8,128)(2,1)S(1)}, u32[]{:S(2)}, u32[]{:S(2)}) async-start(bf16[4,32,256]{2,1,0:T(8,128)(2,1)} %convert_element_type.70), calls=%async_computation | async-start | bytes 131072 | tf_op jit(solution)/shard_map/all_to_all | solution.py:146
  58.0 0.3 fusion.49
  58.4 0.7 copy.124
  59.1 4.7 %collective-permute-start.5 = (bf16[64,256]{1,0:T(8,128)(2,1)}, bf16[64,256]{1,0:T(8,128)(2,1)}, u32[]{:S(2)}, u32[]{:S(2)}) collective-permute-start(bf16[64,256]{1,0:T(8,128)(2,1)} %collective-permute-done.4), channel_id=1, source_target_pairs={{0,28},{4,0},{8,4},{12,8},{16,12},{20,16},{24,20},{28,24},{1,29},{... | collective-permute-start | bytes 98312 | tf_op jit(solution)/shard_map/ppermute | solution.py:119
  63.8 0.6 copy.132
  64.5 0.6 copy.131
  65.1 1.3 %fusion.48 = (f32[128,2,4]{0,2,1:T(4,128)S(1)}, f32[128,2,4,128]{0,3,2,1:T(8,128)S(1)}) fusion(bf16[128,2,128,1]{0,2,3,1:T(8,128)(2,1)} %bitcast.39, bf16[128,2,4,64]{3,0,2,1:T(8,128)(2,1)} %bitcast.100, bf16[128,2,4,64]{3,0,2,1:T(8,128)(2,1)S(1)} %bitcast.97, pred[128,128]{0,1:T(8,128)(4,1)S(1)} %get-tuple-element.68), kind=kOutput, calls=%fused_computation.105 | convolution fusion | flops 34470912 | bytes 872448 | tf_op jit(solution)/shard_map/bgrd,kgd->bgrk/dot_general | solution.py:75
  66.5 0.6 fusion.44
  67.1 1.3 %fusion.2 = f32[128,2,4]{0,2,1:T(4,128)} fusion(f32[2,128,4,512]{3,1,2,0:T(8,128)S(1)} %get-tuple-element.76, f32[128,2,4]{0,2,1:T(4,128)S(1)} %get-tuple-element.66, pred[128,512]{1,0:T(8,128)(4,1)S(1)} %broadcast_compare_fusion), kind=kLoop, calls=%fused_computation.5 | loop fusion | flops 2620416 | bytes 2170880 | tf_op jit(solution)/shard_map/while/body/eval_jaxpr/reduce_sum | solution.py:83
  68.4 1.0 %copy.108 = bf16[128,256]{0,1:T(8,128)(2,1)S(1)} copy(bf16[128,256]{1,0:T(8,128)(2,1)} %collective-permute-done.8) | data formatting | bytes 131072 | tf_op jit(solution)/shard_map/ppermute | solution.py:15
  69.3 1.0 %convolution_bitcast_fusion = f32[128,2,4,128]{0,3,2,1:T(8,128)} fusion(bf16[128,2,128,1]{0,2,3,1:T(8,128)(2,1)S(1)} %bitcast.104, f32[128,2,4,128]{0,3,2,1:T(8,128)S(1)} %get-tuple-element.72, f32[128,2,4]{0,2,1:T(4,128)S(1)} %get-tuple-element.55, pred[128,128]{0,1:T(8,128)(4,1)S(1)} %get-tuple-element.68), kind=kOutput, calls=%fused_computation.7 | convolution fusion | flops 33947648 | bytes 1134592 | tf_op jit(solution)/shard_map/bgrk,kgd->bgrd/dot_general | solution.py:84
  70.4 1.1 %convolution_bitcast_fusion.1 = f32[128,2,4,128]{0,3,2,1:T(8,128)} fusion(bf16[128,2,128,1]{0,2,3,1:T(8,128)(2,1)S(1)} %bitcast.103, f32[128,2,4,128]{0,3,2,1:T(8,128)S(1)} %get-tuple-element.74, f32[128,2,4]{0,2,1:T(4,128)S(1)} %get-tuple-element.56, pred[128,128]{0,1:T(8,128)(4,1)S(1)} %get-tuple-element.67), kind=kOutput, calls=%fused_computation.8 | convolution fusion | flops 33947648 | bytes 1134592 | tf_op jit(solution)/shard_map/bgrk,kgd->bgrd/dot_general | solution.py:84
  71.4 0.1 fusion.23
  71.6 0.1 fusion.21
  71.7 6.7 %collective-permute-done.2 = bf16[64,256]{1,0:T(8,128)(2,1)S(1)} collective-permute-done((bf16[64,256]{1,0:T(8,128)(2,1)}, bf16[64,256]{1,0:T(8,128)(2,1)S(1)}, u32[]{:S(2)}, u32[]{:S(2)}) %collective-permute-start.2) | collective-permute-done | bytes 32800 | tf_op jit(solution)/shard_map/ppermute | solution.py:116
  78.5 4.8 %collective-permute-start.6 = (bf16[64,256]{1,0:T(8,128)(2,1)}, bf16[64,256]{1,0:T(8,128)(2,1)S(1)}, u32[]{:S(2)}, u32[]{:S(2)}) collective-permute-start(bf16[64,256]{1,0:T(8,128)(2,1)} %collective-permute-done.5), channel_id=1, source_target_pairs={{0,28},{4,0},{8,4},{12,8},{16,12},{20,16},{24,20},{28,24},{1,29},{... | collective-permute-start | bytes 98312 | tf_op jit(solution)/shard_map/ppermute | solution.py:119
  83.2 1.8 %collective-permute-done.3 = bf16[64,256]{1,0:T(8,128)(2,1)S(1)} collective-permute-done((bf16[64,256]{1,0:T(8,128)(2,1)S(1)}, bf16[64,256]{1,0:T(8,128)(2,1)S(1)}, u32[]{:S(2)}, u32[]{:S(2)}) %collective-permute-start.3) | collective-permute-done | bytes 32800 | tf_op jit(solution)/shard_map/ppermute | solution.py:116
  85.1 0.8 constant_dynamic-update-slice_fusion.13
  85.8 0.8 constant_dynamic-update-slice_fusion.12
  86.6 0.8 constant_dynamic-update-slice_fusion.10
  87.3 0.8 constant_dynamic-update-slice_fusion.9
  88.1 0.8 constant_dynamic-update-slice_fusion.5
  88.9 0.8 constant_dynamic-update-slice_fusion.4
  89.7 0.8 constant_dynamic-update-slice_fusion.2
  90.4 0.8 constant_dynamic-update-slice_fusion.1
  91.2 0.1 copy.100
  91.4 1.9 %fusion.14 = bf16[128,2,4,128]{0,3,2,1:T(8,128)(2,1)S(1)} fusion(f32[128,2,4,128]{0,3,2,1:T(8,128)} %convolution_bitcast_fusion, f32[128,2,4,128]{0,3,2,1:T(8,128)S(1)} %copy-done.1, bf16[512,2,128,1]{0,2,3,1:T(8,128)(2,1)S(1)} %bitcast.105, f32[2,128,4,512]{3,1,2,0:T(8,128)S(1)} %get-tuple-element.76, f32[128,2,4]{0,2,1:T(4,128)S(1)} %get-tuple-element.66, ...), kind=kOutput, calls=%fused_computation.22 | convolution fusion | flops 137756672 | bytes 3756032 | tf_op jit(solution)/shard_map/while/body/eval_jaxpr/bgrk,kgd->bgrd/dot_general | solution.py:84
  93.3 0.9 copy.113
  (54 shorter events, 1.1 us)
Async XLA Ops:
  0.6 51.4 %copy-start.2 = (bf16[128,1024]{1,0:T(8,128)(2,1)S(1)}, bf16[128,1024]{1,0:T(8,128)(2,1)}, u32[]{:S(2)}) copy-start(bf16[128,1024]{1,0:T(8,128)(2,1)} %param.8) | copy-start | bytes 786436
  0.6 58.5 %collective-permute-start = (bf16[64,256]{1,0:T(8,128)(2,1)}, bf16[64,256]{1,0:T(8,128)(2,1)}, u32[]{:S(2)}, u32[]{:S(2)}) collective-permute-start(bf16[64,256]{1,0:T(8,128)(2,1)} %param.12), channel_id=1, source_target_pairs={{0,4},{4,8},{8,12},{12,16},{16,20},{20,24},{24,28},{28,0},{1,5},{5... | collective-permute-start | bytes 98312 | tf_op jit(solution)/shard_map/ppermute | solution.py:116
  3.6 55.5 %collective-permute-start.4 = (bf16[64,256]{1,0:T(8,128)(2,1)}, bf16[64,256]{1,0:T(8,128)(2,1)}, u32[]{:S(2)}, u32[]{:S(2)}) collective-permute-start(bf16[64,256]{1,0:T(8,128)(2,1)} %param.12), channel_id=1, source_target_pairs={{0,28},{4,0},{8,4},{12,8},{16,12},{20,16},{24,20},{28,24},{1,29},{... | collective-permute-start | bytes 98312 | tf_op jit(solution)/shard_map/ppermute | solution.py:119
  6.7 61.6 %collective-permute-start.8 = (bf16[128,256]{1,0:T(8,128)(2,1)}, bf16[128,256]{1,0:T(8,128)(2,1)}, u32[]{:S(2)}, u32[]{:S(2)}) collective-permute-start(bf16[128,256]{1,0:T(8,128)(2,1)} %param.10), channel_id=1, source_target_pairs={{0,4},{4,8},{8,12},{12,16},{16,20},{20,24},{24,28},{1,5},{5,9},{9,... | collective-permute-start | bytes 196616 | tf_op jit(solution)/shard_map/ppermute | solution.py:15
  8.6 46.1 %all-to-all-start.1 = ((bf16[4,32,256]{2,1,0:T(8,128)(2,1)}), bf16[4,32,256]{2,1,0:T(8,128)(2,1)S(1)}, u32[]{:S(2)}, u32[]{:S(2)}) async-start(bf16[4,32,256]{2,1,0:T(8,128)(2,1)} %bitcast.107), calls=%async_computation.1 | async-start | bytes 131072 | tf_op jit(solution)/shard_map/all_to_all | solution.py:147
  16.7 48.4 %collective-permute-start.7 = (bf16[128,256]{0,1:T(8,128)(2,1)}, bf16[128,256]{0,1:T(8,128)(2,1)}, u32[]{:S(2)}, u32[]{:S(2)}) collective-permute-start(bf16[128,256]{0,1:T(8,128)(2,1)} %bitcast.19), channel_id=1, source_target_pairs={{0,4},{4,8},{8,12},{12,16},{16,20},{20,24},{24,28},{1,5},{5,9},{9,... | collective-permute-start | bytes 196616 | tf_op jit(solution)/shard_map/ppermute | solution.py:15
  52.0 0.7 copy-start.7
  53.1 5.2 %copy-start = (bf16[128,8,64]{2,0,1:T(8,128)(2,1)}, bf16[128,8,64]{2,0,1:T(8,128)(2,1)S(1)}, u32[]{:S(2)}) copy-start(bf16[128,8,64]{2,0,1:T(8,128)(2,1)S(1)} %get-tuple-element.58) | copy-start | bytes 393220
  53.1 5.2 %copy-start.4 = (bf16[128,256]{1,0:T(8,128)(2,1)S(1)}, bf16[128,256]{1,0:T(8,128)(2,1)}, u32[]{:S(2)}) copy-start(bf16[128,256]{1,0:T(8,128)(2,1)} %param.10) | copy-start | bytes 196612
  54.7 9.8 %all-to-all-start = ((bf16[4,32,256]{2,1,0:T(8,128)(2,1)}), bf16[4,32,256]{2,1,0:T(8,128)(2,1)S(1)}, u32[]{:S(2)}, u32[]{:S(2)}) async-start(bf16[4,32,256]{2,1,0:T(8,128)(2,1)} %convert_element_type.70), calls=%async_computation | async-start | bytes 131072 | tf_op jit(solution)/shard_map/all_to_all | solution.py:146
  59.1 12.5 %collective-permute-start.1 = (bf16[64,256]{1,0:T(8,128)(2,1)}, bf16[64,256]{1,0:T(8,128)(2,1)}, u32[]{:S(2)}, u32[]{:S(2)}) collective-permute-start(bf16[64,256]{1,0:T(8,128)(2,1)} %collective-permute-done), channel_id=1, source_target_pairs={{0,4},{4,8},{8,12},{12,16},{16,20},{20,24},{24,28},{28,0},{1,5},{5... | collective-permute-start | bytes 98312 | tf_op jit(solution)/shard_map/ppermute | solution.py:116
  59.1 19.4 %collective-permute-start.5 = (bf16[64,256]{1,0:T(8,128)(2,1)}, bf16[64,256]{1,0:T(8,128)(2,1)}, u32[]{:S(2)}, u32[]{:S(2)}) collective-permute-start(bf16[64,256]{1,0:T(8,128)(2,1)} %collective-permute-done.4), channel_id=1, source_target_pairs={{0,28},{4,0},{8,4},{12,8},{16,12},{20,16},{24,20},{28,24},{1,29},{... | collective-permute-start | bytes 98312 | tf_op jit(solution)/shard_map/ppermute | solution.py:119
  66.5 3.9 %copy-start.3 = (bf16[128,256]{0,1:T(8,128)(2,1)S(1)}, bf16[128,256]{0,1:T(8,128)(2,1)}, u32[]{:S(2)}) copy-start(bf16[128,256]{0,1:T(8,128)(2,1)} %copy.124) | copy-start | bytes 196612
  68.4 18.2 %copy-start.5 = (bf16[64,256]{1,0:T(8,128)(2,1)S(1)}, bf16[64,256]{1,0:T(8,128)(2,1)}, u32[]{:S(2)}) copy-start(bf16[64,256]{1,0:T(8,128)(2,1)} %param.12) | copy-start | bytes 98308
  69.3 9.1 %copy-start.6 = (f32[128,2,4]{0,2,1:T(4,128)S(1)}, f32[128,2,4]{0,2,1:T(4,128)}, u32[]{:S(2)}) copy-start(f32[128,2,4]{0,2,1:T(4,128)} %fusion.2) | copy-start | bytes 12292
  71.5 19.8 %copy-start.1 = (f32[128,2,4,128]{0,3,2,1:T(8,128)S(1)}, f32[128,2,4,128]{0,3,2,1:T(8,128)}, u32[]{:S(2)}) copy-start(f32[128,2,4,128]{0,3,2,1:T(8,128)} %convolution_bitcast_fusion.1) | copy-start | bytes 1572868
  71.6 6.9 %collective-permute-start.2 = (bf16[64,256]{1,0:T(8,128)(2,1)}, bf16[64,256]{1,0:T(8,128)(2,1)S(1)}, u32[]{:S(2)}, u32[]{:S(2)}) collective-permute-start(bf16[64,256]{1,0:T(8,128)(2,1)} %collective-permute-done.1), channel_id=1, source_target_pairs={{0,4},{4,8},{8,12},{12,16},{16,20},{20,24},{24,28},{28,0},{1,5},{5... | collective-permute-start | bytes 98312 | tf_op jit(solution)/shard_map/ppermute | solution.py:116
  78.4 6.6 %collective-permute-start.3 = (bf16[64,256]{1,0:T(8,128)(2,1)S(1)}, bf16[64,256]{1,0:T(8,128)(2,1)S(1)}, u32[]{:S(2)}, u32[]{:S(2)}) collective-permute-start(bf16[64,256]{1,0:T(8,128)(2,1)S(1)} %collective-permute-done.2), channel_id=1, source_target_pairs={{0,4},{4,8},{8,12},{12,16},{16,20},{20,24},{24,28},{28,0},{1,5},{5... | collective-permute-start | bytes 98312 | tf_op jit(solution)/shard_map/ppermute | solution.py:116
  78.5 9.6 %collective-permute-start.6 = (bf16[64,256]{1,0:T(8,128)(2,1)}, bf16[64,256]{1,0:T(8,128)(2,1)S(1)}, u32[]{:S(2)}, u32[]{:S(2)}) collective-permute-start(bf16[64,256]{1,0:T(8,128)(2,1)} %collective-permute-done.5), channel_id=1, source_target_pairs={{0,28},{4,0},{8,4},{12,8},{16,12},{20,16},{24,20},{28,24},{1,29},{... | collective-permute-start | bytes 98312 | tf_op jit(solution)/shard_map/ppermute | solution.py:119
